TPU v7x, 512 devices: a whole 4x8x8 slice. The times are simulated.
512 devices in a mesh: grp: 16 (over y, core), dom: 32 (over x, z).
Axes of the slice: x: 4, y: 8, z: 8, core: 2. Of those that a mesh axis runs over, the one named last changes fastest.
Arguments:
- owned_blips: bfloat16 [2048, 32768], P(('grp', 'dom')), may hold values from -6 to 6
- potential: float32 [32, 512, 1024], P('dom', 'grp'), may hold values from -5 to 5
- slot_owner: int32 [12288, 1], P(('grp', 'dom')), may hold values from 0 to 31; in each aligned block of 24 rows (0 to 23, 24 to 47, ...) at most 2 rows name the same one
- slot_row: int32 [12288], P(('grp', 'dom')), may hold values from 0 to 3
- slot_offset: int32 [12288], P(('grp', 'dom')), may hold values from 0 to 31
Outputs:
- blip_gradient: float32 [2048, 32768], P(('grp', 'dom'))
- hamiltonian: float32 [2048, 128], P(('grp', 'dom'))
Inputs may be any that keep to these rules, and one draw needn't show every extreme that they name: `slot_owner`: among the 24 pieces of one device at most 2 name the same owner.
All inputs are finite; a program needn't handle non-finite values.
Results may differ from a plain program's by a relative error of at most 0.012.
The roundings to bfloat16 on the way count: a program that leaves them out, or rounds other values in their place, can miss the bound.
Values may be sent and summed in bfloat16 or wider, within the bound.
No kernel may reach another device: no remote copies, remote signals or barrier semaphores. Data moves between devices by JAX's collectives and lax.ppermute only.
A program may use at most 128 MiB of HBM per device.

v0:
```python
import jax
import jax.numpy as jnp
from jax import lax
from jax.sharding import PartitionSpec as P

NB = 32


def passed_along(block, axis, distance):
    devices = range(lax.axis_size(axis))
    route = [((i - distance) % len(devices), i) for i in devices]
    return lax.ppermute(block, axis, route)


def spline_tables():
    cells_line = jnp.arange(NB, dtype=jnp.int32)
    offset = cells_line[:, None] - cells_line[None, :]
    spline = jnp.where(
        offset == 0, 2.0 / 3.0, jnp.where(jnp.abs(offset) == 1, 1.0 / 6.0, 0.0)
    ).astype(jnp.float32)
    second = jnp.where(offset == 0, -2.0, jnp.where(jnp.abs(offset) == 1, 1.0, 0.0)).astype(
        jnp.float32
    )
    plane_value = jnp.einsum("ac,bd->abcd", spline, spline).reshape(NB * NB, NB * NB)
    plane_curve = (
        jnp.einsum("ac,bd->abcd", second, spline) + jnp.einsum("ac,bd->abcd", spline, second)
    ).reshape(NB * NB, NB * NB)
    return (
        spline.astype(jnp.bfloat16),
        second.astype(jnp.bfloat16),
        plane_value.astype(jnp.bfloat16),
        plane_curve.astype(jnp.bfloat16),
    )


def on_device(owned_blips, potential, slot_owner, slot_row, slot_offset):
    spline, second, plane_value, plane_curve = spline_tables()
    domain_count = lax.axis_size("dom")
    slot_count = slot_row.shape[0]
    owned_count = owned_blips.shape[0]
    cell_count = owned_blips.shape[1]
    plane_cells = NB * NB
    capacity = max(2, -(-slot_count // domain_count))
    group_size = domain_count * owned_count
    owner_of = slot_owner[:, 0]
    target = owner_of * owned_count + slot_row
    owner_hot = (owner_of[:, None] == jnp.arange(domain_count, dtype=jnp.int32)[None, :]).astype(
        jnp.int32
    )
    position = jnp.sum(jnp.cumsum(owner_hot, axis=0) * owner_hot, axis=1) - 1
    place_slot = owner_of * capacity + position
    place_hot = place_slot[None, :] == jnp.arange(domain_count * capacity, dtype=jnp.int32)[:, None]
    asked_rows = jnp.sum(jnp.where(place_hot, slot_row[None, :], 0), axis=1) + owned_count * (
        1 - jnp.sum(place_hot.astype(jnp.int32), axis=1)
    )
    place_low = place_hot.astype(jnp.bfloat16)
    gathered_rows = lax.all_gather(owned_blips, "dom", axis=0, tiled=True)
    chosen = (
        target[:, None] == jnp.arange(gathered_rows.shape[0], dtype=jnp.int32)[None, :]
    ).astype(jnp.bfloat16)
    slot_blips = jnp.dot(chosen, gathered_rows, preferred_element_type=jnp.float32).astype(
        jnp.bfloat16
    )
    upper_cells = passed_along(potential, "grp", -1)
    extended = jnp.concatenate([potential[0], upper_cells[0]], axis=0)

    def cut_window(first_row):
        return lax.dynamic_slice_in_dim(extended, first_row, NB, 0)

    window = jax.vmap(cut_window)(slot_offset)
    layered = slot_blips.reshape(slot_count, NB, plane_cells)
    y_value = jnp.einsum("ya,sab->syb", spline, layered, preferred_element_type=jnp.float32).astype(
        jnp.bfloat16
    )
    y_curve = jnp.einsum("ya,sab->syb", second, layered, preferred_element_type=jnp.float32).astype(
        jnp.bfloat16
    )
    flat_value = y_value.reshape(-1, plane_cells)
    values_grid = jnp.dot(flat_value, plane_value, preferred_element_type=jnp.float32)
    laplace = jnp.dot(
        y_curve.reshape(-1, plane_cells), plane_value, preferred_element_type=jnp.float32
    ) + jnp.dot(flat_value, plane_curve, preferred_element_type=jnp.float32)
    applied = (-0.5 * laplace + window.reshape(-1, plane_cells) * values_grid).astype(jnp.bfloat16)
    values_low = values_grid.astype(jnp.bfloat16)
    back_plane = jnp.dot(applied, plane_value, preferred_element_type=jnp.float32).astype(
        jnp.bfloat16
    )
    gradient_piece = jnp.einsum(
        "ay,sab->syb",
        spline,
        back_plane.reshape(slot_count, NB, plane_cells),
        preferred_element_type=jnp.float32,
    ).astype(jnp.bfloat16)
    intersection = lax.dot_general(
        values_low.reshape(slot_count, cell_count),
        applied.reshape(slot_count, cell_count),
        (((1,), (1,)), ((), ())),
        preferred_element_type=jnp.float32,
    ) / float(cell_count)
    select_full = (target[:, None] == jnp.arange(group_size, dtype=jnp.int32)[None, :]).astype(
        jnp.float32
    )
    weighted = jnp.dot(intersection, select_full, precision=lax.Precision.HIGHEST)
    part_hot = (
        target[:, None] == jnp.arange(owned_count * lax.axis_size("dom"), dtype=jnp.int32)[None, :]
    ).astype(jnp.float32)
    hamilton = lax.psum_scatter(
        jnp.dot(part_hot.T, weighted, precision=lax.Precision.HIGHEST),
        "dom",
        scatter_dimension=0,
        tiled=True,
    )
    send_grad = jnp.dot(
        place_low,
        gradient_piece.reshape(slot_count, cell_count),
        preferred_element_type=jnp.bfloat16,
    ).reshape(domain_count, capacity, cell_count)
    got_grad, got_rows = (
        lax.all_to_all(send_grad, "dom", split_axis=0, concat_axis=0, tiled=True),
        lax.all_to_all(
            asked_rows.reshape(domain_count, capacity),
            "dom",
            split_axis=0,
            concat_axis=0,
            tiled=True,
        ),
    )
    owner_pick = (
        got_rows.reshape(-1)[None, :] == jnp.arange(owned_count, dtype=jnp.int32)[:, None]
    ).astype(jnp.bfloat16)
    gradient = jnp.dot(
        owner_pick, got_grad.reshape(-1, cell_count), preferred_element_type=jnp.float32
    )
    return (gradient, hamilton)


def solution(mesh):
    placed = (
        P(("grp", "dom"), None),
        P("dom", "grp", None),
        P(("grp", "dom"), None),
        P(("grp", "dom")),
        P(("grp", "dom")),
    )
    return jax.shard_map(
        on_device,
        mesh=mesh,
        in_specs=placed,
        out_specs=(P(("grp", "dom"), None), P(("grp", "dom"), None)),
        check_vma=False,
    )
```

profile of v0, /device:TPU:2, one launch (start us, length us, event | category | flops | bytes accessed | tf_op | source)
XLA Modules:
  0.0 352.7 jit_solution(15724551003374242884)
XLA Ops:
  7.9 2.9 collective-permute-start
  14.6 13.5 %all-to-all-start = ((s32[32,1,2]{2,1,0:T(1,128)}), s32[32,1,2]{2,1,0:T(1,128)S(1)}, u32[]{:S(2)}, u32[]{:S(2)}) async-start(s32[32,1,2]{2,1,0:T(1,128)} %bitcast.1), calls=%async_computation | async-start | bytes 32768 | tf_op jit(solution)/shard_map/all_to_all | solution.py:120
  28.2 7.6 %fusion.1 = (bf16[32,32,32,32]{3,2,1,0:T(8,128)(2,1)}, bf16[32,32,32,32]{3,2,1,0:T(8,128)(2,1)}) fusion(f32[32,32]{1,0:T(8,128)S(1)} %copy.33, f32[32,32]{1,0:T(8,128)S(1)} %copy.30), kind=kLoop, calls=%fused_computation.6 | loop fusion | flops 6291456 | bytes 4202496 | tf_op jit(solution)/shard_map/convert_element_type | solution.py:32
  35.9 12.4 %convert_element_type.78 = bf16[1024,1024]{1,0:T(8,128)(2,1)} reshape(bf16[32,32,32,32]{3,2,1,0:T(8,128)(2,1)} %get-tuple-element.21) | data formatting | bytes 4194304 | tf_op jit(solution)/shard_map/convert_element_type | solution.py:31
  48.3 11.4 %convert_element_type.84 = bf16[1024,1024]{1,0:T(8,128)(2,1)S(1)} reshape(bf16[32,32,32,32]{3,2,1,0:T(8,128)(2,1)} %get-tuple-element.20) | data formatting | bytes 4194304 | tf_op jit(solution)/shard_map/convert_element_type | solution.py:32
  59.8 48.0 %while.1 = (s32[]{:T(128)}, f32[64,1024]{1,0:T(8,128)S(1)}, s32[24,2]{0,1:T(2,128)S(1)}, f32[24,32,1024]{2,1,0:T(8,128)}, s32[]{:T(128)}) while((s32[]{:T(128)}, f32[64,1024]{1,0:T(8,128)S(1)}, s32[24,2]{0,1:T(2,128)S(1)}, f32[24,32,1024]{2,1,0:T(8,128)}, s32[]{:T(128)}) %tuple.24), condition=%wide.while_cond, body=%wide.while_body.sunk | while | flops 2 | bytes 263257 | solution.py:68
  60.4 1.3 bitcast_dynamic-update-slice_fusion.2
  64.4 1.3 bitcast_dynamic-update-slice_fusion.2
  66.4 1.4 bitcast_dynamic-update-slice_fusion.2
  70.4 1.3 bitcast_dynamic-update-slice_fusion.2
  72.4 1.3 bitcast_dynamic-update-slice_fusion.2
  78.4 1.3 bitcast_dynamic-update-slice_fusion.2
  82.4 1.4 bitcast_dynamic-update-slice_fusion.2
  84.4 1.3 bitcast_dynamic-update-slice_fusion.2
  90.4 1.4 bitcast_dynamic-update-slice_fusion.2
  96.4 1.3 bitcast_dynamic-update-slice_fusion.2
  100.4 1.3 bitcast_dynamic-update-slice_fusion.2
  104.4 1.3 bitcast_dynamic-update-slice_fusion.2
  107.7 10.9 %all-gather.3.cloned.1.call-done = bf16[32,4,32768]{2,1,0:T(4,128)(2,1)} async-done(((bf16[1,4,32768]{2,1,0:T(4,128)(2,1)}), bf16[32,4,32768]{2,1,0:T(4,128)(2,1)}) %all-gather.3.cloned.1.call-update) | async-done | bytes 8388624 | tf_op jit(solution)/shard_map/all_gather | solution.py:57
  118.6 12.7 %reshape.131 = bf16[128,32768]{1,0:T(8,128)(2,1)} reshape(bf16[32,4,32768]{2,1,0:T(4,128)(2,1)} %all-gather.3.cloned.1.call-done) | data formatting | bytes 16777216
  131.3 4.6 %convolution_convert_fusion = bf16[24,32768]{1,0:T(8,128)(2,1)S(1)} fusion(bf16[128,32768]{1,0:T(8,128)(2,1)} %reshape.131, s32[24]{0:T(128)S(1)} %get-tuple-element.23), kind=kOutput, calls=%fused_computation.2 | convolution fusion | flops 202116096 | bytes 9961568 | tf_op jit(solution)/shard_map/dot_general | solution.py:61
  139.0 3.0 fusion.41
  142.1 1.8 fusion.42
  143.9 1.9 fusion.3
  145.9 1.8 convolution_convert_fusion.4
  149.2 1.4 fusion.5
  150.6 6.3 %copy.35 = bf16[32,2,32768]{2,1,0:T(2,128)(2,1)} copy(bf16[32,2,32768]{2,0,1:T(8,128)(2,1)S(1)} %fusion.5) | data formatting | bytes 8388608 | tf_op jit(solution)/shard_map/dot_general | solution.py:113
  156.9 7.2 %all-to-all-start.1 = ((bf16[32,2,32768]{2,1,0:T(2,128)(2,1)}), bf16[32,2,32768]{2,1,0:T(2,128)(2,1)}, u32[]{:S(2)}, u32[]{:S(2)}) async-start(bf16[32,2,32768]{2,1,0:T(2,128)(2,1)} %copy.35), calls=%async_computation.1 | async-start | bytes 8388608 | tf_op jit(solution)/shard_map/all_to_all | solution.py:119
  164.9 2.6 reshape.109
  172.6 161.1 %all-reduce.4.cloned.1.call-done = f32[128,128]{1,0:T(8,128)} async-done(((f32[128,128]{1,0:T(8,128)}), f32[128,128]{1,0:T(8,128)}) %all-reduce.4.cloned.1.call-update) | async-done | bytes 65552
  334.9 7.3 %reshape.108 = bf16[64,32768]{1,0:T(8,128)(2,1)} reshape(bf16[32,2,32768]{2,1,0:T(2,128)(2,1)} %all-to-all-done.1) | data formatting | bytes 8388608 | tf_op jit(solution)/shard_map/reshape | solution.py:132
  342.2 3.6 %fusion.23 = f32[4,32768]{1,0:T(4,128)} fusion(bf16[64,32768]{1,0:T(8,128)(2,1)} %reshape.108, s32[64]{0:T(128)S(1)} %eq.115), kind=kOutput, calls=%fused_computation.45 | convolution fusion | flops 16777472 | bytes 4718848 | tf_op jit(solution)/shard_map/dot_general | solution.py:131
  (109 shorter events, 47.6 us)
Async XLA Ops:
  7.2 111.5 %all-gather.3.cloned.1.call-start = ((), (), s32[]{:S(2)}) async-start(), calls=%async_computation.2 | async-start | bytes 8650752 | tf_op jit(solution)/shard_map/all_gather | solution.py:57
  7.9 51.8 %collective-permute-start = (f32[1,32,1024]{2,1,0:T(8,128)}, f32[1,32,1024]{2,1,0:T(8,128)S(1)}, u32[]{:S(2)}, u32[]{:S(2)}) collective-permute-start(f32[1,32,1024]{2,1,0:T(8,128)} %param.6), channel_id=1, source_target_pairs={{32,0},{64,32},{96,64},{128,96},{160,128},{192,160},{224,192},{256... | collective-permute-start | bytes 393224 | tf_op jit(solution)/shard_map/ppermute | solution.py:12
  14.6 142.3 %all-to-all-start = ((s32[32,1,2]{2,1,0:T(1,128)}), s32[32,1,2]{2,1,0:T(1,128)S(1)}, u32[]{:S(2)}, u32[]{:S(2)}) async-start(s32[32,1,2]{2,1,0:T(1,128)} %bitcast.1), calls=%async_computation | async-start | bytes 32768 | tf_op jit(solution)/shard_map/all_to_all | solution.py:120
  28.2 7.6 %copy-start.5 = (s32[24]{0:T(128)S(1)}, s32[24]{0:T(128)}, u32[]{:S(2)}) copy-start(s32[24]{0:T(128)} %param.9) | copy-start | bytes 292
  48.3 11.4 %copy-start.4 = (f32[1,32,1024]{2,1,0:T(8,128)S(1)}, f32[1,32,1024]{2,1,0:T(8,128)}, u32[]{:S(2)}) copy-start(f32[1,32,1024]{2,1,0:T(8,128)} %param.6) | copy-start | bytes 393220
  137.4 1.6 copy-start.3
  142.1 1.9 copy-start.2
  145.9 1.8 copy-start
  156.9 7.3 %copy-start.1 = (bf16[768,1024]{1,0:T(8,128)(2,1)S(1)}, bf16[768,1024]{1,0:T(8,128)(2,1)}, u32[]{:S(2)}) copy-start(bf16[768,1024]{1,0:T(8,128)(2,1)} %copy-done) | copy-start | bytes 4718596
  156.9 178.1 %all-to-all-start.1 = ((bf16[32,2,32768]{2,1,0:T(2,128)(2,1)}), bf16[32,2,32768]{2,1,0:T(2,128)(2,1)}, u32[]{:S(2)}, u32[]{:S(2)}) async-start(bf16[32,2,32768]{2,1,0:T(2,128)(2,1)} %copy.35), calls=%async_computation.1 | async-start | bytes 8388608 | tf_op jit(solution)/shard_map/all_to_all | solution.py:119
  164.1 169.6 %all-reduce.4.cloned.1.call-start = ((), (), s32[]{:S(2)}) async-start(), calls=%async_computation.3 | async-start | bytes 131072
Sparse Core Ops, SparseCore 0:
  11.1 107.4 all-gather.2
  169.4 164.1 all-reduce.3
where the time goes:
time: 354 us; the launch traced here: 353 us
  waiting for transfers between devices  173 us (49%)
  local copies, waits for them, and re-layouts  108 us (31%)
  starting transfers between devices  23.7 us (7%)
  matrix products  21.8 us (6%)
  between operations  14.9 us (4%)
  other arithmetic  11.4 us (3%)
    unnamed x3, waiting for transfers between devices  162 us
    gather x72, local copies, waits for them, and re-layouts  47.9 us
    unnamed x16, local copies, waits for them, and re-layouts  17.1 us
    all_to_all x1, starting transfers between devices, on_device(): lax.all_to_all(asked_rows.reshape(domain_count, capacity), 'dom', split_a...  13.5 us
    convert_element_type x1, local copies, waits for them, and re-layouts, spline_tables(): plane_value.astype(jnp.bfloat16)  12.4 us
    convert_element_type x1, local copies, waits for them, and re-layouts, spline_tables(): plane_curve.astype(jnp.bfloat16)  11.4 us
    all_gather x1, waiting for transfers between devices, on_device(): gathered_rows = lax.all_gather(owned_blips, 'dom', axis=0, tiled=True)  10.9 us
    convert_element_type x1, other arithmetic, spline_tables(): plane_curve.astype(jnp.bfloat16)  7.61 us
  transfers between devices with their start and end apart: 5, of which 2 were waited for; matrix products, arithmetic and copies ran while one was open for 37% of the time, Pallas kernels for 0%

commit v1 on v0

--- a/solution.py
+++ b/solution.py
@@ -1,9 +1,19 @@
+import functools
 import jax
 import jax.numpy as jnp
 from jax import lax
 from jax.sharding import PartitionSpec as P
 
 NB = 32
+
+
+def divide_sectors_now(work_x, row_dim):
+    later = lax.axis_size("dom")
+    state_next = jnp.concatenate([work_x] * later, axis=row_dim)
+    return lax.all_to_all(state_next, "dom", row_dim, row_dim, tiled=True)
+
+
+spread_steps_all = functools.partial(divide_sectors_now, row_dim=0)
 
 
 def passed_along(block, axis, distance):
@@ -54,7 +64,7 @@
         1 - jnp.sum(place_hot.astype(jnp.int32), axis=1)
     )
     place_low = place_hot.astype(jnp.bfloat16)
-    gathered_rows = lax.all_gather(owned_blips, "dom", axis=0, tiled=True)
+    gathered_rows = spread_steps_all(owned_blips)
     chosen = (
         target[:, None] == jnp.arange(gathered_rows.shape[0], dtype=jnp.int32)[None, :]
     ).astype(jnp.bfloat16)

time: 354 us -> 527 us (1.49)
  waiting for transfers between devices: 173 us -> 261 us
  local copies, waits for them, and re-layouts: 108 us -> 175 us
  starting transfers between devices: 23.7 us -> 40.5 us
    all_to_all x0 -> x1, waiting for transfers between devices: none -> 101 us  [divide_sectors_now(): return lax.all_to_all(state_next, 'dom', row_dim, row_dim, tiled=True)]
    concatenate x0 -> x1, local copies, waits for them, and re-layouts: none -> 53.4 us  [divide_sectors_now(): state_next = jnp.concatenate([work_x] * later, axis=row_dim)]
    all_to_all x0 -> x2, local copies, waits for them, and re-layouts: none -> 25.7 us  [divide_sectors_now(): return lax.all_to_all(state_next, 'dom', row_dim, row_dim, tiled=True)]
    all_to_all x0 -> x1, starting transfers between devices: none -> 13.7 us  [divide_sectors_now(): return lax.all_to_all(state_next, 'dom', row_dim, row_dim, tiled=True)]
    unnamed x16 -> x19, local copies, waits for them, and re-layouts: 17.1 us -> 4.41 us
    all_gather x1 -> x0, waiting for transfers between devices: 10.9 us -> none  [on_device(): gathered_rows = lax.all_gather(owned_blips, 'dom', axis=0, tiled=True)]
    unnamed x3 -> x2, waiting for transfers between devices: 162 us -> 160 us
  transfers between devices with their start and end apart: 5 -> 5, of which waited for: 2 -> 2; matrix products, arithmetic and copies ran while one was open for 37% -> 22% of each run, Pallas kernels for 0% -> 0%
where the time goes in v1:
time: 527 us; the launch traced here: 522 us
  waiting for transfers between devices  261 us (50%)
  local copies, waits for them, and re-layouts  175 us (33%)
  starting transfers between devices  40.5 us (8%)
  matrix products  21.8 us (4%)
  between operations  14.9 us (3%)
  other arithmetic  8.72 us (2%)
    unnamed x2, waiting for transfers between devices  160 us
    all_to_all x1, waiting for transfers between devices, divide_sectors_now(): return lax.all_to_all(state_next, 'dom', row_dim, row_dim, tiled=True)  101 us
    concatenate x1, local copies, waits for them, and re-layouts, divide_sectors_now(): state_next = jnp.concatenate([work_x] * later, axis=row_dim)  53.4 us
    gather x72, local copies, waits for them, and re-layouts  48.4 us
    all_to_all x2, local copies, waits for them, and re-layouts, divide_sectors_now(): return lax.all_to_all(state_next, 'dom', row_dim, row_dim, tiled=True)  25.7 us
    all_to_all x1, starting transfers between devices, on_device(): lax.all_to_all(asked_rows.reshape(domain_count, capacity), 'dom', split_a...  14.4 us
    all_to_all x1, starting transfers between devices, divide_sectors_now(): return lax.all_to_all(state_next, 'dom', row_dim, row_dim, tiled=True)  13.7 us
    convert_element_type x1, local copies, waits for them, and re-layouts, spline_tables(): plane_value.astype(jnp.bfloat16)  12.4 us
  transfers between devices with their start and end apart: 5, of which 2 were waited for; matrix products, arithmetic and copies ran while one was open for 22% of the time, Pallas kernels for 0%

profile of v1, /device:TPU:2, one launch (start us, length us, event | category | flops | bytes accessed | tf_op | source)
XLA Modules:
  0.0 522.4 jit_solution(16077072969938248982)
XLA Ops:
  7.2 53.4 %concatenate.9 = bf16[128,32768]{1,0:T(8,128)(2,1)} concatenate(bf16[4,32768]{1,0:T(4,128)(2,1)} %param.5, bf16[4,32768]{1,0:T(4,128)(2,1)} %param.5, bf16[4,32768]{1,0:T(4,128)(2,1)} %param.5, bf16[4,32768]{1,0:T(4,128)(2,1)} %param.5, bf16[4,32768]{1,0:T(4,128)(2,1)} %param.5, bf16[4,32768]{1,0:T(4,128)(2,1)} %param.5, bf16[4,32768]{1,0:T(4,128)(2,1)} %param.5, ...), dimensions={0} | concatenate | bytes 16777216 | tf_op jit(solution)/shard_map/concatenate | solution.py:12
  60.6 13.0 %all_to_all.16 = bf16[32,4,32768]{2,1,0:T(4,128)(2,1)} reshape(bf16[128,32768]{1,0:T(8,128)(2,1)} %concatenate.9) | data formatting | bytes 16777216 | tf_op jit(solution)/shard_map/all_to_all | solution.py:13
  73.6 13.7 %all-to-all-start.1 = ((bf16[32,4,32768]{2,1,0:T(4,128)(2,1)}), bf16[32,4,32768]{2,1,0:T(4,128)(2,1)}, u32[]{:S(2)}, u32[]{:S(2)}) async-start(bf16[32,4,32768]{2,1,0:T(4,128)(2,1)} %all_to_all.16), calls=%async_computation.1 | async-start | bytes 16777216 | tf_op jit(solution)/shard_map/all_to_all | solution.py:13
  87.3 2.4 collective-permute-start
  90.3 7.6 %fusion.1 = (bf16[32,32,32,32]{3,2,1,0:T(8,128)(2,1)}, bf16[32,32,32,32]{3,2,1,0:T(8,128)(2,1)}) fusion(f32[32,32]{1,0:T(8,128)S(1)} %copy.33, f32[32,32]{1,0:T(8,128)S(1)} %copy.30), kind=kLoop, calls=%fused_computation.6 | loop fusion | flops 6291456 | bytes 4202496 | tf_op jit(solution)/shard_map/convert_element_type | solution.py:42
  97.9 12.4 %convert_element_type.78 = bf16[1024,1024]{1,0:T(8,128)(2,1)} reshape(bf16[32,32,32,32]{3,2,1,0:T(8,128)(2,1)} %get-tuple-element.21) | data formatting | bytes 4194304 | tf_op jit(solution)/shard_map/convert_element_type | solution.py:41
  110.3 11.3 %convert_element_type.84 = bf16[1024,1024]{1,0:T(8,128)(2,1)S(1)} reshape(bf16[32,32,32,32]{3,2,1,0:T(8,128)(2,1)} %get-tuple-element.20) | data formatting | bytes 4194304 | tf_op jit(solution)/shard_map/convert_element_type | solution.py:42
  122.4 48.5 %while.1 = (s32[]{:T(128)}, f32[64,1024]{1,0:T(8,128)S(1)}, s32[24,2]{0,1:T(2,128)S(1)}, f32[24,32,1024]{2,1,0:T(8,128)}, s32[]{:T(128)}) while((s32[]{:T(128)}, f32[64,1024]{1,0:T(8,128)S(1)}, s32[24,2]{0,1:T(2,128)S(1)}, f32[24,32,1024]{2,1,0:T(8,128)}, s32[]{:T(128)}) %tuple.24), condition=%wide.while_cond, body=%wide.while_body.sunk | while | flops 2 | bytes 263257 | solution.py:78
  129.1 1.4 bitcast_dynamic-update-slice_fusion.2
  133.1 1.4 bitcast_dynamic-update-slice_fusion.2
  135.1 1.4 bitcast_dynamic-update-slice_fusion.2
  137.2 1.4 bitcast_dynamic-update-slice_fusion.2
  139.2 1.4 bitcast_dynamic-update-slice_fusion.2
  151.3 1.4 bitcast_dynamic-update-slice_fusion.2
  155.3 1.4 bitcast_dynamic-update-slice_fusion.2
  159.4 1.4 bitcast_dynamic-update-slice_fusion.2
  161.4 1.4 bitcast_dynamic-update-slice_fusion.2
  163.4 1.4 bitcast_dynamic-update-slice_fusion.2
  170.8 101.2 %all-to-all-done.1 = bf16[32,4,32768]{2,1,0:T(4,128)(2,1)} async-done(((bf16[32,4,32768]{2,1,0:T(4,128)(2,1)}), bf16[32,4,32768]{2,1,0:T(4,128)(2,1)}, u32[]{:S(2)}, u32[]{:S(2)}) %all-to-all-start.1) | async-done | bytes 8388640 | tf_op jit(solution)/shard_map/all_to_all | solution.py:13
  272.0 14.4 %all-to-all-start = ((s32[32,1,2]{2,1,0:T(1,128)}), s32[32,1,2]{2,1,0:T(1,128)S(1)}, u32[]{:S(2)}, u32[]{:S(2)}) async-start(s32[32,1,2]{2,1,0:T(1,128)} %bitcast.1), calls=%async_computation | async-start | bytes 32768 | tf_op jit(solution)/shard_map/all_to_all | solution.py:130
  286.5 12.7 %all_to_all.18 = bf16[128,32768]{1,0:T(8,128)(2,1)} reshape(bf16[32,4,32768]{2,1,0:T(4,128)(2,1)} %all-to-all-done.1) | data formatting | bytes 16777216 | tf_op jit(solution)/shard_map/all_to_all | solution.py:13
  299.1 4.6 convolution_convert_fusion
  306.9 3.0 fusion.41
  309.9 1.8 fusion.42
  311.8 1.9 fusion.3
  313.7 1.8 convolution_convert_fusion.4
  318.5 6.3 %copy.35 = bf16[32,2,32768]{2,1,0:T(2,128)(2,1)} copy(bf16[32,2,32768]{2,0,1:T(8,128)(2,1)S(1)} %fusion.5) | data formatting | bytes 8388608 | tf_op jit(solution)/shard_map/dot_general | solution.py:123
  324.8 10.0 %all-to-all-start.2 = ((bf16[32,2,32768]{2,1,0:T(2,128)(2,1)}), bf16[32,2,32768]{2,1,0:T(2,128)(2,1)}, u32[]{:S(2)}, u32[]{:S(2)}) async-start(bf16[32,2,32768]{2,1,0:T(2,128)(2,1)} %copy.35), calls=%async_computation.2 | async-start | bytes 8388608 | tf_op jit(solution)/shard_map/all_to_all | solution.py:129
  335.6 2.6 reshape.111
  343.2 160.2 %all-reduce.4.cloned.1.call-done = f32[128,128]{1,0:T(8,128)} async-done(((f32[128,128]{1,0:T(8,128)}), f32[128,128]{1,0:T(8,128)}) %all-reduce.4.cloned.1.call-update) | async-done | bytes 65552
  504.7 7.3 %reshape.110 = bf16[64,32768]{1,0:T(8,128)(2,1)} reshape(bf16[32,2,32768]{2,1,0:T(2,128)(2,1)} %all-to-all-done.2) | data formatting | bytes 8388608 | tf_op jit(solution)/shard_map/reshape | solution.py:142
  512.0 3.6 fusion.23
  (114 shorter events, 48.7 us)
Async XLA Ops:
  73.6 13.7 %copy-start.4 = (f32[1,32,1024]{2,1,0:T(8,128)S(1)}, f32[1,32,1024]{2,1,0:T(8,128)}, u32[]{:S(2)}) copy-start(f32[1,32,1024]{2,1,0:T(8,128)} %param.6) | copy-start | bytes 393220
  73.6 16.2 %copy-start.5 = (s32[24,1]{0,1:T(1,128)S(1)}, s32[24,1]{0,1:T(1,128)}, u32[]{:S(2)}) copy-start(s32[24,1]{0,1:T(1,128)} %param.7) | copy-start | bytes 292
  73.6 16.5 %copy-start.6 = (s32[24]{0:T(128)S(1)}, s32[24]{0:T(128)}, u32[]{:S(2)}) copy-start(s32[24]{0:T(128)} %param.8) | copy-start | bytes 292
  73.6 198.4 %all-to-all-start.1 = ((bf16[32,4,32768]{2,1,0:T(4,128)(2,1)}), bf16[32,4,32768]{2,1,0:T(4,128)(2,1)}, u32[]{:S(2)}, u32[]{:S(2)}) async-start(bf16[32,4,32768]{2,1,0:T(4,128)(2,1)} %all_to_all.16), calls=%async_computation.1 | async-start | bytes 16777216 | tf_op jit(solution)/shard_map/all_to_all | solution.py:13
  87.3 35.0 %collective-permute-start = (f32[1,32,1024]{2,1,0:T(8,128)S(1)}, f32[1,32,1024]{2,1,0:T(8,128)S(1)}, u32[]{:S(2)}, u32[]{:S(2)}) collective-permute-start(f32[1,32,1024]{2,1,0:T(8,128)S(1)} %copy-done.4), channel_id=1, source_target_pairs={{32,0},{64,32},{96,64},{128,96},{160,128},{192,160},{224,192},{256... | collective-permute-start | bytes 393224 | tf_op jit(solution)/shard_map/ppermute | solution.py:22
  90.3 7.6 %copy-start.7 = (s32[24]{0:T(128)S(1)}, s32[24]{0:T(128)}, u32[]{:S(2)}) copy-start(s32[24]{0:T(128)} %param.9) | copy-start | bytes 292
  272.0 52.7 %all-to-all-start = ((s32[32,1,2]{2,1,0:T(1,128)}), s32[32,1,2]{2,1,0:T(1,128)S(1)}, u32[]{:S(2)}, u32[]{:S(2)}) async-start(s32[32,1,2]{2,1,0:T(1,128)} %bitcast.1), calls=%async_computation | async-start | bytes 32768 | tf_op jit(solution)/shard_map/all_to_all | solution.py:130
  305.3 1.6 copy-start.3
  309.9 1.9 copy-start.2
  313.7 1.8 copy-start
  324.8 10.0 %copy-start.1 = (bf16[768,1024]{1,0:T(8,128)(2,1)S(1)}, bf16[768,1024]{1,0:T(8,128)(2,1)}, u32[]{:S(2)}) copy-start(bf16[768,1024]{1,0:T(8,128)(2,1)} %copy-done) | copy-start | bytes 4718596
  324.8 179.9 %all-to-all-start.2 = ((bf16[32,2,32768]{2,1,0:T(2,128)(2,1)}), bf16[32,2,32768]{2,1,0:T(2,128)(2,1)}, u32[]{:S(2)}, u32[]{:S(2)}) async-start(bf16[32,2,32768]{2,1,0:T(2,128)(2,1)} %copy.35), calls=%async_computation.2 | async-start | bytes 8388608 | tf_op jit(solution)/shard_map/all_to_all | solution.py:129
  334.7 168.7 %all-reduce.4.cloned.1.call-start = ((), (), s32[]{:S(2)}) async-start(), calls=%async_computation.3 | async-start | bytes 131072
Sparse Core Ops, SparseCore 0:
  340.1 163.2 all-reduce.3
